TPU v7x, 256 devices: a whole 4x4x8 slice. The times are simulated.
256 devices in a mesh: hyp: 32 (over y, x, core), head: 8 (over z).
Axes of the slice: x: 4, y: 4, z: 8, core: 2. Of those that a mesh axis runs over, the one named last changes fastest.
Arguments:
- step_embeds: bfloat16 [3, 512, 4096], P(None, 'hyp'), may hold values from -6 to 6
- lang_table: bfloat16 [8, 4096], replicated, may hold values from -3 to 3
- lang_ids: int32 [32, 4], replicated, may hold values from 0 to 7
- self_gain: float32 [4096], replicated, may hold values from 0.1 to 1.9
- self_wq: bfloat16 [4096, 2048], P(None, 'head'), may hold values from -0.09375 to 0.09375
- self_wk: bfloat16 [4096, 2048], P(None, 'head'), may hold values from -0.09375 to 0.09375
- self_wv: bfloat16 [4096, 2048], P(None, 'head'), may hold values from -0.09375 to 0.09375
- self_wo: bfloat16 [2048, 4096], P('head'), may hold values from -0.125 to 0.125
- cross_gain: float32 [4096], replicated, may hold values from 0.1 to 1.9
- cross_wq: bfloat16 [4096, 2048], P(None, 'head'), may hold values from -0.09375 to 0.09375
- cross_wkv: bfloat16 [4096, 4096], P('hyp', 'head'), may hold values from -0.09375 to 0.09375
- encoder_rows: bfloat16 [24576, 4096], P('hyp', 'head'), may hold values from -200 to 200
- doc_lengths: int32 [32], P('hyp'), may hold values from 192 to 768, as said below
- past_keys: bfloat16 [512, 32, 2048], P('hyp', None, 'head'), may hold values from -200 to 200
- past_values: bfloat16 [512, 32, 2048], P('hyp', None, 'head'), may hold values from -6 to 6
- parents: int32 [3, 512], replicated, may hold values from 0 to 3
Outputs:
- cross_context: bfloat16 [3, 512, 2048], P(None, 'hyp', 'head')
- final_keys: bfloat16 [512, 35, 2048], P('hyp', None, 'head')
- final_values: bfloat16 [512, 35, 2048], P('hyp', None, 'head')
Inputs may be any that keep to these rules, and one draw needn't show every extreme that they name: `doc_lengths`: some document has exactly 768 live rows. `parents`: A parent is a beam of the same document and target.
All inputs are finite; a program needn't handle non-finite values.
Results may differ from a plain program's by a relative error of at most 0.03.
Values may be sent and summed in bfloat16 or wider, within the bound.
No kernel may reach another device: no remote copies, remote signals or barrier semaphores. Data moves between devices by JAX's collectives and lax.ppermute only.
A program may use at most 128 MiB of HBM per device.

v0:
```python
import jax
import jax.numpy as jnp
from jax import lax
from jax.sharding import PartitionSpec as P

HEAD = 256
BEAMS = 4
TARGETS = 4
STEPS = 3
EPSILON = 1e-06


def rms_scaled(values_in, gain):
    mean_square = jnp.mean(values_in * values_in, axis=-1, keepdims=True)
    return values_in * lax.rsqrt(mean_square + EPSILON) * gain


def pick_rows(candidates, selector, row_axis):
    shape_list = [1] * candidates[0].ndim
    shape_list[row_axis] = selector.shape[0]
    chosen = candidates[0]
    for position in range(1, len(candidates)):
        chosen = jnp.where((selector == position).reshape(shape_list), candidates[position], chosen)
    return chosen


def beam_copies(block, hyp_count, group_size):
    copies = [block]
    for hop in range(1, BEAMS):
        distance = hop * group_size
        route = [((i - distance) % hyp_count, i) for i in range(hyp_count)]
        copies.append(lax.ppermute(block, "hyp", route))
    return copies


def cross_attend(queries, cross_keys, cross_values, doc_length, scaling):
    scores = (
        jnp.einsum("qd,jd->qj", queries, cross_keys, preferred_element_type=jnp.float32) * scaling
    )
    live_mask = lax.broadcasted_iota(jnp.int32, (1, cross_keys.shape[0]), 1) < doc_length
    scores = jnp.where(live_mask, scores, -jnp.inf)
    highest = jnp.max(scores, axis=1, keepdims=True)
    raw_weights = jnp.exp(scores - highest)
    totals = jnp.sum(raw_weights, axis=1, keepdims=True)
    weights = (raw_weights / totals).astype(jnp.bfloat16)
    output = jnp.einsum("qj,jd->qd", weights, cross_values, preferred_element_type=jnp.float32)
    return output.astype(jnp.bfloat16)


def shards(
    step_embeds,
    lang_table,
    lang_ids,
    self_gain,
    self_wq,
    self_wk,
    self_wv,
    self_wo,
    cross_gain,
    cross_wq,
    cross_wkv,
    encoder_rows,
    doc_lengths,
    past_keys,
    past_values,
    parents,
):
    hyp_count = lax.axis_size("hyp")
    group_size = hyp_count // BEAMS
    my_index = lax.axis_index("hyp")
    my_beam = my_index // group_size
    my_slot = my_index % group_size
    steps = step_embeds.shape[0]
    row_count = step_embeds.shape[1]
    docs_here = row_count // TARGETS
    head_width = self_wq.shape[1]
    doc_count = lang_ids.shape[0]
    past_len = past_keys.shape[1]
    scaling = HEAD ** (-0.5)
    full_weights = lax.all_gather(cross_wkv, "hyp", axis=0, tiled=True)
    full_rows = lax.all_gather(encoder_rows, "head", axis=1, tiled=True)
    cross_kv = jnp.dot(full_rows, full_weights, preferred_element_type=jnp.float32).astype(
        jnp.bfloat16
    )
    cross_kv = cross_kv.reshape(encoder_rows.shape[0], 2, HEAD)
    cross_keys = cross_kv[:, 0, :]
    cross_values = cross_kv[:, 1, :]
    doc_length = doc_lengths[0]
    past_stack = jnp.stack([past_keys, past_values])
    past_all = beam_copies(past_stack, hyp_count, group_size)
    my_langs = lax.dynamic_slice_in_dim(lang_ids, my_slot * docs_here, docs_here, 0).reshape(
        row_count
    )
    one_hot = (
        my_langs[:, None] == lax.broadcasted_iota(jnp.int32, (1, lang_table.shape[0]), 1)
    ).astype(jnp.bfloat16)
    lang_rows = jnp.dot(one_hot, lang_table, preferred_element_type=jnp.float32)
    hidden_in = step_embeds.astype(jnp.float32) + lang_rows[None]
    normed = rms_scaled(hidden_in, self_gain).astype(jnp.bfloat16).reshape(steps * row_count, -1)
    new_query = jnp.dot(normed, self_wq, preferred_element_type=jnp.float32).astype(jnp.bfloat16)
    new_key = jnp.dot(normed, self_wk, preferred_element_type=jnp.float32).astype(jnp.bfloat16)
    new_value = jnp.dot(normed, self_wv, preferred_element_type=jnp.float32).astype(jnp.bfloat16)
    new_query = new_query.reshape(steps, row_count, head_width)
    fresh = jnp.stack([new_key, new_value]).reshape(2, steps, row_count, head_width)
    fresh_all = beam_copies(fresh, hyp_count, group_size)
    parent_view = parents.reshape(steps, BEAMS, doc_count * TARGETS)
    parent_of = lax.dynamic_slice_in_dim(parent_view, my_slot * row_count, row_count, 2)
    own_beam = jnp.full((row_count,), my_beam, jnp.int32)

    def hop_of(beam):
        return (my_beam - beam) % BEAMS

    def climb(step_idx, beam):
        return jnp.take_along_axis(parent_of[step_idx], beam[None, :], axis=0)[0]

    def cache_at(step_idx):
        ancestor = own_beam
        new_parts = [None] * (step_idx + 1)
        new_parts[step_idx] = fresh[:, step_idx]
        for back in range(step_idx, 0, -1):
            ancestor = climb(back, ancestor)
            new_parts[back - 1] = pick_rows(
                [f[:, back - 1] for f in fresh_all], hop_of(ancestor), 1
            )
        ancestor = climb(0, ancestor)
        past_part = pick_rows(past_all, hop_of(ancestor), 1)
        return jnp.concatenate([past_part] + [n[:, :, None, :] for n in new_parts], axis=2)

    contexts = []
    final_cache = None
    for step_idx in range(steps):
        cache = cache_at(step_idx)
        if step_idx == steps - 1:
            final_cache = cache
        query = new_query[step_idx]
        scores = (
            jnp.einsum("rd,rpd->rp", query, cache[0], preferred_element_type=jnp.float32) * scaling
        )
        highest = jnp.max(scores, axis=1, keepdims=True)
        raw_weights = jnp.exp(scores - highest)
        totals = jnp.sum(raw_weights, axis=1, keepdims=True)
        summed = jnp.einsum(
            "rp,rpd->rd",
            raw_weights,
            cache[1].astype(jnp.float32),
            preferred_element_type=jnp.float32,
        )
        contexts.append((summed / totals).astype(jnp.bfloat16))
    self_context = jnp.stack(contexts).reshape(steps * row_count, head_width)
    partial_out = jnp.dot(self_context, self_wo, preferred_element_type=jnp.float32)
    summed_out = lax.psum(partial_out.astype(jnp.bfloat16), "head").astype(jnp.float32)
    residual = hidden_in + summed_out.reshape(hidden_in.shape)
    normed_cross = rms_scaled(residual, cross_gain).astype(jnp.bfloat16)
    cross_query = jnp.dot(
        normed_cross.reshape(steps * row_count, -1), cross_wq, preferred_element_type=jnp.float32
    ).astype(jnp.bfloat16)
    by_doc = cross_query.reshape(steps, docs_here, TARGETS, head_width)
    sent = []
    for shift in range(BEAMS):
        route = [
            (beam * group_size + slot, slot * docs_here + (beam + shift) % BEAMS)
            for beam in range(BEAMS)
            for slot in range(group_size)
        ]
        piece = lax.dynamic_index_in_dim(by_doc, (my_beam + shift) % BEAMS, 1, keepdims=False)
        sent.append(lax.ppermute(piece, "hyp", route))
    doc_queries = jnp.stack(sent).reshape(BEAMS * steps * TARGETS, head_width)
    answer = cross_attend(doc_queries, cross_keys, cross_values, doc_length, scaling)
    answer = answer.reshape(BEAMS, steps, TARGETS, head_width)
    back = []
    for shift in range(BEAMS):
        route = [
            (slot * docs_here + (beam + shift) % BEAMS, beam * group_size + slot)
            for beam in range(BEAMS)
            for slot in range(group_size)
        ]
        back.append(lax.ppermute(answer[shift], "hyp", route))
    back = jnp.stack(back)
    order = (jnp.arange(docs_here, dtype=jnp.int32) - my_beam) % BEAMS
    by_k = jnp.take(back, order, axis=0)
    contexts_out = by_k.transpose(1, 0, 2, 3).reshape(steps, row_count, head_width)
    return (contexts_out, final_cache[0], final_cache[1])


def solution(mesh):
    return jax.shard_map(
        shards,
        mesh=mesh,
        in_specs=(
            P(None, "hyp", None),
            P(),
            P(),
            P(),
            P(None, "head"),
            P(None, "head"),
            P(None, "head"),
            P("head", None),
            P(),
            P(None, "head"),
            P("hyp", "head"),
            P("hyp", "head"),
            P("hyp"),
            P("hyp", None, "head"),
            P("hyp", None, "head"),
            P(),
        ),
        out_specs=(P(None, "hyp", "head"), P("hyp", None, "head"), P("hyp", None, "head")),
        check_vma=False,
    )
```

profile of v0, /device:TPU:17, one launch (start us, length us, event | category | flops | bytes accessed | tf_op | source)
XLA Modules:
  0.0 224.9 jit_solution(5241141596806689058)
XLA Ops:
  10.2 1.3 multiply_reduce_fusion.1
  12.8 2.1 convolution_convert_fusion.4
  15.6 2.6 %collective-permute-start.4 = (bf16[2,3,16,256]{3,2,0,1:T(8,128)(2,1)S(1)}, bf16[2,3,16,256]{3,2,0,1:T(8,128)(2,1)S(1)}, u32[]{:S(2)}, u32[]{:S(2)}) collective-permute-start(bf16[2,3,16,256]{3,2,0,1:T(8,128)(2,1)S(1)} %pad_maximum_fusion.4), channel_id=1, source_target_pairs={{128,0},{136,8},{144,16},{152,24},{160,32},{168,40},{176,48},{184,... | collective-permute-start | bytes 147464 | tf_op jit(solution)/shard_map/ppermute | solution.py:32
  19.4 1.5 collective-permute-start
  20.9 1.6 collective-permute-start.1
  25.1 1.2 gather_fusion.5
  32.0 2.1 convolution_convert_fusion.6
  34.7 11.1 %collective-permute-done.2 = bf16[2,16,32,256]{3,1,2,0:T(8,128)(2,1)S(1)} collective-permute-done((bf16[2,16,32,256]{3,1,2,0:T(8,128)(2,1)}, bf16[2,16,32,256]{3,1,2,0:T(8,128)(2,1)S(1)}, u32[]{:S(2)}, u32[]{:S(2)}) %collective-permute-start.2) | collective-permute-done | bytes 524320 | tf_op jit(solution)/shard_map/ppermute | solution.py:32
  45.8 1.5 select_select_fusion.2
  50.2 1.2 convolution_convert_fusion
  53.4 78.1 %all-reduce.2.cloned.1.call-done = bf16[3,16,4096]{2,1,0:T(8,128)(2,1)} async-done(((bf16[3,16,4096]{2,1,0:T(8,128)(2,1)}), bf16[3,16,4096]{2,1,0:T(8,128)(2,1)}) %all-reduce.2.cloned.1.call-update) | async-done | bytes 393232 | tf_op jit(solution)/shard_map/psum | solution.py:151
  131.6 1.4 multiply_reduce_fusion
  134.7 4.6 %collective-permute-start.9 = (bf16[3,4,256]{2,1,0:T(4,128)(2,1)S(1)}, bf16[3,4,256]{2,1,0:T(4,128)(2,1)S(1)}, u32[]{:S(2)}, u32[]{:S(2)}) collective-permute-start(bf16[3,4,256]{2,1,0:T(4,128)(2,1)S(1)} %get-tuple-element.43), channel_id=1, source_target_pairs={{0,24},{8,56},{16,88},{24,120},{32,152},{40,184},{48,216},{56,248}... | collective-permute-start | bytes 18440 | tf_op jit(solution)/shard_map/ppermute | solution.py:166
  139.3 12.5 %collective-permute-start.8 = (bf16[3,4,256]{2,1,0:T(4,128)(2,1)S(1)}, bf16[3,4,256]{2,1,0:T(4,128)(2,1)S(1)}, u32[]{:S(2)}, u32[]{:S(2)}) collective-permute-start(bf16[3,4,256]{2,1,0:T(4,128)(2,1)S(1)} %get-tuple-element.44), channel_id=1, source_target_pairs={{0,16},{8,48},{16,80},{24,112},{32,144},{40,176},{48,208},{56,240}... | collective-permute-start | bytes 18440 | tf_op jit(solution)/shard_map/ppermute | solution.py:166
  151.8 5.5 %collective-permute-start.7 = (bf16[3,4,256]{2,1,0:T(4,128)(2,1)S(1)}, bf16[3,4,256]{2,1,0:T(4,128)(2,1)S(1)}, u32[]{:S(2)}, u32[]{:S(2)}) collective-permute-start(bf16[3,4,256]{2,1,0:T(4,128)(2,1)S(1)} %get-tuple-element.45), channel_id=1, source_target_pairs={{0,8},{8,40},{16,72},{24,104},{32,136},{40,168},{48,200},{56,232},... | collective-permute-start | bytes 18440 | tf_op jit(solution)/shard_map/ppermute | solution.py:166
  157.3 3.3 %collective-permute-start.6 = (bf16[3,4,256]{2,1,0:T(4,128)(2,1)S(1)}, bf16[3,4,256]{2,1,0:T(4,128)(2,1)S(1)}, u32[]{:S(2)}, u32[]{:S(2)}) collective-permute-start(bf16[3,4,256]{2,1,0:T(4,128)(2,1)S(1)} %get-tuple-element.42), channel_id=1, source_target_pairs={{0,0},{8,32},{16,64},{24,96},{32,128},{40,160},{48,192},{56,224},{... | collective-permute-start | bytes 18440 | tf_op jit(solution)/shard_map/ppermute | solution.py:166
  160.6 4.0 %collective-permute-done.6 = bf16[3,4,256]{2,1,0:T(4,128)(2,1)S(1)} collective-permute-done((bf16[3,4,256]{2,1,0:T(4,128)(2,1)S(1)}, bf16[3,4,256]{2,1,0:T(4,128)(2,1)S(1)}, u32[]{:S(2)}, u32[]{:S(2)}) %collective-permute-start.6) | collective-permute-done | bytes 6176 | tf_op jit(solution)/shard_map/ppermute | solution.py:166
  164.7 21.2 %all-gather.3.cloned.1.call-done = bf16[768,4096]{1,0:T(8,128)(2,1)} async-done(((bf16[768,512]{1,0:T(8,128)(2,1)}), bf16[768,4096]{1,0:T(8,128)(2,1)}) %all-gather.3.cloned.1.call-update) | async-done | bytes 6291472 | tf_op jit(solution)/shard_map/all_gather | solution.py:81
  186.0 7.5 %convolution_convert_fusion.1 = bf16[768,512]{0,1:T(8,128)(2,1)S(1)} fusion(bf16[768,4096]{1,0:T(8,128)(2,1)} %all-gather.3.cloned.1.call-done, bf16[4096,512]{1,0:T(8,128)(2,1)} %all-gather.5.cloned.1.call-done), kind=kOutput, calls=%fused_computation.8 | convolution fusion | flops 3221618688 | bytes 11272192 | tf_op jit(solution)/shard_map/dot_general | solution.py:82
  194.3 5.6 %collective-permute-start.13 = (bf16[3,4,256]{2,1,0:T(4,128)(2,1)S(1)}, bf16[3,4,256]{2,1,0:T(4,128)(2,1)S(1)}, u32[]{:S(2)}, u32[]{:S(2)}) collective-permute-start(bf16[3,4,256]{2,1,0:T(4,128)(2,1)S(1)} %squeeze.124), channel_id=1, source_target_pairs={{24,0},{56,8},{88,16},{120,24},{152,32},{184,40},{216,48},{248,56}... | collective-permute-start | bytes 18440 | tf_op jit(solution)/shard_map/ppermute | solution.py:177
  199.9 1.7 collective-permute-start.12
  201.7 5.9 %collective-permute-start.11 = (bf16[3,4,256]{2,1,0:T(4,128)(2,1)S(1)}, bf16[3,4,256]{2,1,0:T(4,128)(2,1)S(1)}, u32[]{:S(2)}, u32[]{:S(2)}) collective-permute-start(bf16[3,4,256]{2,1,0:T(4,128)(2,1)S(1)} %squeeze.122), channel_id=1, source_target_pairs={{8,0},{40,8},{72,16},{104,24},{136,32},{168,40},{200,48},{232,56},... | collective-permute-start | bytes 18440 | tf_op jit(solution)/shard_map/ppermute | solution.py:177
  207.6 2.9 %collective-permute-start.10 = (bf16[3,4,256]{2,1,0:T(4,128)(2,1)S(1)}, bf16[3,4,256]{2,1,0:T(4,128)(2,1)S(1)}, u32[]{:S(2)}, u32[]{:S(2)}) collective-permute-start(bf16[3,4,256]{2,1,0:T(4,128)(2,1)S(1)} %squeeze.121), channel_id=1, source_target_pairs={{0,0},{32,8},{64,16},{96,24},{128,32},{160,40},{192,48},{224,56},{... | collective-permute-start | bytes 18440 | tf_op jit(solution)/shard_map/ppermute | solution.py:177
  210.6 5.6 %collective-permute-done.10 = bf16[3,4,256]{2,1,0:T(4,128)(2,1)S(1)} collective-permute-done((bf16[3,4,256]{2,1,0:T(4,128)(2,1)S(1)}, bf16[3,4,256]{2,1,0:T(4,128)(2,1)S(1)}, u32[]{:S(2)}, u32[]{:S(2)}) %collective-permute-start.10) | collective-permute-done | bytes 6176 | tf_op jit(solution)/shard_map/ppermute | solution.py:177
  (140 shorter events, 22.1 us)
Async XLA Ops:
  8.0 42.2 %copy-start = (bf16[256,4096]{1,0:T(8,128)(2,1)S(1)}, bf16[256,4096]{1,0:T(8,128)(2,1)}, u32[]{:S(2)}) copy-start(bf16[256,4096]{1,0:T(8,128)(2,1)} %param.25) | copy-start | bytes 6291460
  8.0 123.5 %all-reduce.2.cloned.1.call-start = ((), (), s32[]{:S(2)}) async-start(), calls=%async_computation | async-start | bytes 786432 | tf_op jit(solution)/shard_map/psum | solution.py:151
  10.2 4.7 %copy-start.2 = (bf16[4096,256]{1,0:T(8,128)(2,1)S(1)}, bf16[4096,256]{1,0:T(8,128)(2,1)}, u32[]{:S(2)}) copy-start(bf16[4096,256]{1,0:T(8,128)(2,1)} %param.23) | copy-start | bytes 6291460
  12.7 5.5 %copy-start.6 = (bf16[16,32,256]{2,1,0:T(8,128)(2,1)S(1)}, bf16[16,32,256]{2,1,0:T(8,128)(2,1)}, u32[]{:S(2)}) copy-start(bf16[16,32,256]{2,1,0:T(8,128)(2,1)} %param.32) | copy-start | bytes 786436
  12.7 5.5 %copy-start.7 = (bf16[16,32,256]{2,1,0:T(8,128)(2,1)S(1)}, bf16[16,32,256]{2,1,0:T(8,128)(2,1)}, u32[]{:S(2)}) copy-start(bf16[16,32,256]{2,1,0:T(8,128)(2,1)} %param.31) | copy-start | bytes 786436
  14.9 7.5 %copy-start.9 = (s32[3,512]{1,0:T(4,128)S(1)}, s32[3,512]{1,0:T(4,128)}, u32[]{:S(2)}) copy-start(s32[3,512]{1,0:T(4,128)} %param.33) | copy-start | bytes 18436
  15.4 18.8 %collective-permute-start.3 = (bf16[2,3,16,256]{3,2,0,1:T(8,128)(2,1)S(1)}, bf16[2,3,16,256]{3,2,0,1:T(8,128)(2,1)S(1)}, u32[]{:S(2)}, u32[]{:S(2)}) collective-permute-start(bf16[2,3,16,256]{3,2,0,1:T(8,128)(2,1)S(1)} %pad_maximum_fusion.4), channel_id=1, source_target_pairs={{64,0},{72,8},{80,16},{88,24},{96,32},{104,40},{112,48},{120,56},{... | collective-permute-start | bytes 147464 | tf_op jit(solution)/shard_map/ppermute | solution.py:32
  15.6 18.8 %collective-permute-start.4 = (bf16[2,3,16,256]{3,2,0,1:T(8,128)(2,1)S(1)}, bf16[2,3,16,256]{3,2,0,1:T(8,128)(2,1)S(1)}, u32[]{:S(2)}, u32[]{:S(2)}) collective-permute-start(bf16[2,3,16,256]{3,2,0,1:T(8,128)(2,1)S(1)} %pad_maximum_fusion.4), channel_id=1, source_target_pairs={{128,0},{136,8},{144,16},{152,24},{160,32},{168,40},{176,48},{184,... | collective-permute-start | bytes 147464 | tf_op jit(solution)/shard_map/ppermute | solution.py:32
  18.3 16.2 %collective-permute-start.5 = (bf16[2,3,16,256]{3,2,0,1:T(8,128)(2,1)S(1)}, bf16[2,3,16,256]{3,2,0,1:T(8,128)(2,1)S(1)}, u32[]{:S(2)}, u32[]{:S(2)}) collective-permute-start(bf16[2,3,16,256]{3,2,0,1:T(8,128)(2,1)S(1)} %pad_maximum_fusion.4), channel_id=1, source_target_pairs={{192,0},{200,8},{208,16},{216,24},{224,32},{232,40},{240,48},{248,... | collective-permute-start | bytes 147464 | tf_op jit(solution)/shard_map/ppermute | solution.py:32
  19.4 15.3 %collective-permute-start = (bf16[2,16,32,256]{3,1,2,0:T(8,128)(2,1)}, bf16[2,16,32,256]{3,1,2,0:T(8,128)(2,1)}, u32[]{:S(2)}, u32[]{:S(2)}) collective-permute-start(bf16[2,16,32,256]{3,1,2,0:T(8,128)(2,1)} %pad_maximum_fusion.2), channel_id=1, source_target_pairs={{64,0},{72,8},{80,16},{88,24},{96,32},{104,40},{112,48},{120,56},{... | collective-permute-start | bytes 1572872 | tf_op jit(solution)/shard_map/ppermute | solution.py:32
  20.9 13.8 %collective-permute-start.1 = (bf16[2,16,32,256]{3,1,2,0:T(8,128)(2,1)}, bf16[2,16,32,256]{3,1,2,0:T(8,128)(2,1)}, u32[]{:S(2)}, u32[]{:S(2)}) collective-permute-start(bf16[2,16,32,256]{3,1,2,0:T(8,128)(2,1)} %pad_maximum_fusion.2), channel_id=1, source_target_pairs={{128,0},{136,8},{144,16},{152,24},{160,32},{168,40},{176,48},{184,... | collective-permute-start | bytes 1572872 | tf_op jit(solution)/shard_map/ppermute | solution.py:32
  34.2 11.7 %collective-permute-start.2 = (bf16[2,16,32,256]{3,1,2,0:T(8,128)(2,1)}, bf16[2,16,32,256]{3,1,2,0:T(8,128)(2,1)S(1)}, u32[]{:S(2)}, u32[]{:S(2)}) collective-permute-start(bf16[2,16,32,256]{3,1,2,0:T(8,128)(2,1)} %pad_maximum_fusion.2), channel_id=1, source_target_pairs={{192,0},{200,8},{208,16},{216,24},{224,32},{232,40},{240,48},{248,... | collective-permute-start | bytes 1572872 | tf_op jit(solution)/shard_map/ppermute | solution.py:32
  50.1 81.4 %copy-start.1 = (bf16[3,16,4096]{2,1,0:T(8,128)(2,1)S(1)}, bf16[3,16,4096]{2,1,0:T(8,128)(2,1)}, u32[]{:S(2)}) copy-start(bf16[3,16,4096]{2,1,0:T(8,128)(2,1)} %param.18) | copy-start | bytes 1179652
  50.2 82.7 %copy-start.8 = (f32[4096]{0:T(1024)S(1)}, f32[4096]{0:T(1024)}, u32[]{:S(2)}) copy-start(f32[4096]{0:T(1024)} %param.26) | copy-start | bytes 49156
  51.5 113.2 %all-gather.5.cloned.1.call-start = ((), (), s32[]{:S(2)}) async-start(), calls=%async_computation.2 | async-start | bytes 4325376 | tf_op jit(solution)/shard_map/all_gather | solution.py:80
  52.1 133.9 %all-gather.3.cloned.1.call-start = ((), (), s32[]{:S(2)}) async-start(), calls=%async_computation.1 | async-start | bytes 7077888 | tf_op jit(solution)/shard_map/all_gather | solution.py:81
  134.7 25.9 %collective-permute-start.9 = (bf16[3,4,256]{2,1,0:T(4,128)(2,1)S(1)}, bf16[3,4,256]{2,1,0:T(4,128)(2,1)S(1)}, u32[]{:S(2)}, u32[]{:S(2)}) collective-permute-start(bf16[3,4,256]{2,1,0:T(4,128)(2,1)S(1)} %get-tuple-element.43), channel_id=1, source_target_pairs={{0,24},{8,56},{16,88},{24,120},{32,152},{40,184},{48,216},{56,248}... | collective-permute-start | bytes 18440 | tf_op jit(solution)/shard_map/ppermute | solution.py:166
  139.3 21.3 %collective-permute-start.8 = (bf16[3,4,256]{2,1,0:T(4,128)(2,1)S(1)}, bf16[3,4,256]{2,1,0:T(4,128)(2,1)S(1)}, u32[]{:S(2)}, u32[]{:S(2)}) collective-permute-start(bf16[3,4,256]{2,1,0:T(4,128)(2,1)S(1)} %get-tuple-element.44), channel_id=1, source_target_pairs={{0,16},{8,48},{16,80},{24,112},{32,144},{40,176},{48,208},{56,240}... | collective-permute-start | bytes 18440 | tf_op jit(solution)/shard_map/ppermute | solution.py:166
  151.8 8.8 %collective-permute-start.7 = (bf16[3,4,256]{2,1,0:T(4,128)(2,1)S(1)}, bf16[3,4,256]{2,1,0:T(4,128)(2,1)S(1)}, u32[]{:S(2)}, u32[]{:S(2)}) collective-permute-start(bf16[3,4,256]{2,1,0:T(4,128)(2,1)S(1)} %get-tuple-element.45), channel_id=1, source_target_pairs={{0,8},{8,40},{16,72},{24,104},{32,136},{40,168},{48,200},{56,232},... | collective-permute-start | bytes 18440 | tf_op jit(solution)/shard_map/ppermute | solution.py:166
  157.3 7.4 %collective-permute-start.6 = (bf16[3,4,256]{2,1,0:T(4,128)(2,1)S(1)}, bf16[3,4,256]{2,1,0:T(4,128)(2,1)S(1)}, u32[]{:S(2)}, u32[]{:S(2)}) collective-permute-start(bf16[3,4,256]{2,1,0:T(4,128)(2,1)S(1)} %get-tuple-element.42), channel_id=1, source_target_pairs={{0,0},{8,32},{16,64},{24,96},{32,128},{40,160},{48,192},{56,224},{... | collective-permute-start | bytes 18440 | tf_op jit(solution)/shard_map/ppermute | solution.py:166
  194.3 16.3 %collective-permute-start.13 = (bf16[3,4,256]{2,1,0:T(4,128)(2,1)S(1)}, bf16[3,4,256]{2,1,0:T(4,128)(2,1)S(1)}, u32[]{:S(2)}, u32[]{:S(2)}) collective-permute-start(bf16[3,4,256]{2,1,0:T(4,128)(2,1)S(1)} %squeeze.124), channel_id=1, source_target_pairs={{24,0},{56,8},{88,16},{120,24},{152,32},{184,40},{216,48},{248,56}... | collective-permute-start | bytes 18440 | tf_op jit(solution)/shard_map/ppermute | solution.py:177
  199.9 10.7 %collective-permute-start.12 = (bf16[3,4,256]{2,1,0:T(4,128)(2,1)S(1)}, bf16[3,4,256]{2,1,0:T(4,128)(2,1)S(1)}, u32[]{:S(2)}, u32[]{:S(2)}) collective-permute-start(bf16[3,4,256]{2,1,0:T(4,128)(2,1)S(1)} %squeeze.123), channel_id=1, source_target_pairs={{16,0},{48,8},{80,16},{112,24},{144,32},{176,40},{208,48},{240,56}... | collective-permute-start | bytes 18440 | tf_op jit(solution)/shard_map/ppermute | solution.py:177
  201.7 8.9 %collective-permute-start.11 = (bf16[3,4,256]{2,1,0:T(4,128)(2,1)S(1)}, bf16[3,4,256]{2,1,0:T(4,128)(2,1)S(1)}, u32[]{:S(2)}, u32[]{:S(2)}) collective-permute-start(bf16[3,4,256]{2,1,0:T(4,128)(2,1)S(1)} %squeeze.122), channel_id=1, source_target_pairs={{8,0},{40,8},{72,16},{104,24},{136,32},{168,40},{200,48},{232,56},... | collective-permute-start | bytes 18440 | tf_op jit(solution)/shard_map/ppermute | solution.py:177
  207.6 8.6 %collective-permute-start.10 = (bf16[3,4,256]{2,1,0:T(4,128)(2,1)S(1)}, bf16[3,4,256]{2,1,0:T(4,128)(2,1)S(1)}, u32[]{:S(2)}, u32[]{:S(2)}) collective-permute-start(bf16[3,4,256]{2,1,0:T(4,128)(2,1)S(1)} %squeeze.121), channel_id=1, source_target_pairs={{0,0},{32,8},{64,16},{96,24},{128,32},{160,40},{192,48},{224,56},{... | collective-permute-start | bytes 18440 | tf_op jit(solution)/shard_map/ppermute | solution.py:177
  (9 other events, 18.6 us)
Sparse Core Ops, SparseCore 0:
  51.6 79.8 all-reduce.1
Sparse Core Ops, SparseCore 1:
  54.5 55.5 all-gather.4
  111.8 74.1 all-gather.2
where the time goes:
time: 225 us
  waiting for transfers between devices  121 us (54%)
  starting transfers between devices  48.4 us (22%)
  between operations  16.9 us (8%)
  matrix products  16.7 us (7%)
  other arithmetic  13.6 us (6%)
  local copies, waits for them, and re-layouts  8.23 us (4%)
    psum x1, waiting for transfers between devices, shards(): lax.psum(partial_out.astype(jnp.bfloat16), 'head').astype(jnp.float32)  78.1 us
    ppermute x4, starting transfers between devices, shards(): sent.append(lax.ppermute(piece, 'hyp', route))  25.9 us
    all_gather x1, waiting for transfers between devices, shards(): full_rows = lax.all_gather(encoder_rows, 'head', axis=1, tiled=True)  21.2 us
    ppermute x4, starting transfers between devices, shards(): back.append(lax.ppermute(answer[shift], 'hyp', route))  16.2 us
    ppermute x6, waiting for transfers between devices, beam_copies(): copies.append(lax.ppermute(block, 'hyp', route))  11.1 us
    dot_general x1, matrix products, shards(): jnp.dot(full_rows, full_weights, preferred_element_type=jnp.float32)  7.47 us
    ppermute x6, starting transfers between devices, beam_copies(): copies.append(lax.ppermute(block, 'hyp', route))  6.19 us
    ppermute x4, waiting for transfers between devices, shards(): back.append(lax.ppermute(answer[shift], 'hyp', route))  5.57 us
  transfers between devices with their start and end apart: 17, of which 5 were waited for; matrix products, arithmetic and copies ran while one was open for 7% of the time, Pallas kernels for 0%

commit v1 on v0

--- a/solution.py
+++ b/solution.py
@@ -78,7 +78,16 @@
     past_len = past_keys.shape[1]
     scaling = HEAD ** (-0.5)
     full_weights = lax.all_gather(cross_wkv, "hyp", axis=0, tiled=True)
-    full_rows = lax.all_gather(encoder_rows, "head", axis=1, tiled=True)
+    write_streams_up = lambda inner_x, ax_name: jnp.concatenate(
+        jax.lax.all_to_all(
+            jnp.stack([inner_x for _ in range(jax.lax.axis_size(ax_name))]),
+            axis_name=ax_name,
+            split_axis=0,
+            concat_axis=0,
+        ),
+        axis=1,
+    )
+    full_rows = write_streams_up(encoder_rows, "head")
     cross_kv = jnp.dot(full_rows, full_weights, preferred_element_type=jnp.float32).astype(
         jnp.bfloat16
     )

time: 225 us -> 241 us (1.071)
  starting transfers between devices: 48.4 us -> 73.9 us
  waiting for transfers between devices: 121 us -> 108 us
  local copies, waits for them, and re-layouts: 8.23 us -> 11.7 us
    all_gather x1 -> x0, waiting for transfers between devices: 21.2 us -> none  [shards(): full_rows = lax.all_gather(encoder_rows, 'head', axis=1, tiled=True)]
    ppermute x4, starting transfers between devices: 25.9 us -> 46 us  [shards(): sent.append(lax.ppermute(piece, 'hyp', route))]
    psum x1, waiting for transfers between devices: 78.1 us -> 89.3 us  [shards(): lax.psum(partial_out.astype(jnp.bfloat16), 'head').astype(jnp.float32)]
    all_to_all x0 -> x1, starting transfers between devices: none -> 8.32 us  [shards(): jax.lax.all_to_all(jnp.stack([inner_x for _ in range(jax.lax.axis_size(ax...]
    eq x10, other arithmetic: 3.41 us -> 0.12 us  [pick_rows(): selector == position]
    another operation x0 -> x1, local copies, waits for them, and re-layouts: none -> 3.04 us  [shards(): jnp.stack([inner_x for _ in range(jax.lax.axis_size(ax_name))])]
    ppermute x4, starting transfers between devices: 16.2 us -> 13.2 us  [shards(): back.append(lax.ppermute(answer[shift], 'hyp', route))]
  transfers between devices with their start and end apart: 17 -> 17, of which waited for: 5 -> 4; matrix products, arithmetic and copies ran while one was open for 7% -> 9% of each run, Pallas kernels for 0% -> 0%
where the time goes in v1:
time: 241 us; the launch traced here: 239 us
  waiting for transfers between devices  108 us (45%)
  starting transfers between devices  73.9 us (31%)
  between operations  16.9 us (7%)
  matrix products  16.7 us (7%)
  other arithmetic  11.9 us (5%)
  local copies, waits for them, and re-layouts  11.7 us (5%)
    psum x1, waiting for transfers between devices, shards(): lax.psum(partial_out.astype(jnp.bfloat16), 'head').astype(jnp.float32)  89.3 us
    ppermute x4, starting transfers between devices, shards(): sent.append(lax.ppermute(piece, 'hyp', route))  46 us
    ppermute x4, starting transfers between devices, shards(): back.append(lax.ppermute(answer[shift], 'hyp', route))  13.2 us
    ppermute x6, waiting for transfers between devices, beam_copies(): copies.append(lax.ppermute(block, 'hyp', route))  9.42 us
    all_to_all x1, starting transfers between devices, shards(): jax.lax.all_to_all(jnp.stack([inner_x for _ in range(jax.lax.axis_size(ax...  8.32 us
    dot_general x1, matrix products, shards(): jnp.dot(full_rows, full_weights, preferred_element_type=jnp.float32)  7.47 us
    ppermute x6, starting transfers between devices, beam_copies(): copies.append(lax.ppermute(block, 'hyp', route))  6.22 us
    ppermute x4, waiting for transfers between devices, shards(): back.append(lax.ppermute(answer[shift], 'hyp', route))  4.83 us
  transfers between devices with their start and end apart: 17, of which 4 were waited for; matrix products, arithmetic and copies ran while one was open for 9% of the time, Pallas kernels for 0%

profile of v1, /device:TPU:17, one launch (start us, length us, event | category | flops | bytes accessed | tf_op | source)
XLA Modules:
  0.0 239.2 jit_solution(6611355574590929312)
XLA Ops:
  10.2 1.3 multiply_reduce_fusion.1
  12.7 2.1 convolution_convert_fusion.4
  16.1 2.6 %collective-permute-start.4 = (bf16[2,3,16,256]{3,2,0,1:T(8,128)(2,1)}, bf16[2,3,16,256]{3,2,0,1:T(8,128)(2,1)}, u32[]{:S(2)}, u32[]{:S(2)}) collective-permute-start(bf16[2,3,16,256]{3,2,0,1:T(8,128)(2,1)} %pad_maximum_fusion.4), channel_id=1, source_target_pairs={{128,0},{136,8},{144,16},{152,24},{160,32},{168,40},{176,48},{184,... | collective-permute-start | bytes 147464 | tf_op jit(solution)/shard_map/ppermute | solution.py:32
  20.1 1.5 collective-permute-start
  21.5 1.6 collective-permute-start.1
  23.2 1.4 copy.52
  24.6 3.0 %stack.86 = bf16[8,768,512]{1,2,0:T(8,128)(2,1)} broadcast(bf16[768,512]{0,1:T(8,128)(2,1)S(1)} %copy.52), dimensions={1,2} | broadcast | bytes 7077888 | tf_op jit(solution)/shard_map/stack | solution.py:83
  27.6 8.3 %all-to-all-start = ((bf16[8,768,512]{1,2,0:T(8,128)(2,1)}), bf16[8,768,512]{1,2,0:T(8,128)(2,1)}, u32[]{:S(2)}, u32[]{:S(2)}) async-start(bf16[8,768,512]{1,2,0:T(8,128)(2,1)} %stack.86), calls=%async_computation | async-start | bytes 12582912 | tf_op jit(solution)/shard_map/all_to_all | solution.py:82
  40.7 2.1 convolution_convert_fusion.6
  44.9 9.4 %collective-permute-done.2 = bf16[2,16,32,256]{3,1,2,0:T(8,128)(2,1)S(1)} collective-permute-done((bf16[2,16,32,256]{3,1,2,0:T(8,128)(2,1)}, bf16[2,16,32,256]{3,1,2,0:T(8,128)(2,1)S(1)}, u32[]{:S(2)}, u32[]{:S(2)}) %collective-permute-start.2) | collective-permute-done | bytes 524320 | tf_op jit(solution)/shard_map/ppermute | solution.py:32
  54.3 1.5 select_select_fusion.2
  61.3 89.3 %all-reduce.2.cloned.1.call-done = bf16[3,16,4096]{2,1,0:T(8,128)(2,1)} async-done(((bf16[3,16,4096]{2,1,0:T(8,128)(2,1)}), bf16[3,16,4096]{2,1,0:T(8,128)(2,1)}) %all-reduce.2.cloned.1.call-update) | async-done | bytes 393232 | tf_op jit(solution)/shard_map/psum | solution.py:160
  150.6 1.4 multiply_reduce_fusion
  153.7 5.6 %collective-permute-start.9 = (bf16[3,4,256]{2,1,0:T(4,128)(2,1)S(1)}, bf16[3,4,256]{2,1,0:T(4,128)(2,1)S(1)}, u32[]{:S(2)}, u32[]{:S(2)}) collective-permute-start(bf16[3,4,256]{2,1,0:T(4,128)(2,1)S(1)} %get-tuple-element.43), channel_id=1, source_target_pairs={{0,24},{8,56},{16,88},{24,120},{32,152},{40,184},{48,216},{56,248}... | collective-permute-start | bytes 18440 | tf_op jit(solution)/shard_map/ppermute | solution.py:175
  159.3 2.6 %collective-permute-start.8 = (bf16[3,4,256]{2,1,0:T(4,128)(2,1)S(1)}, bf16[3,4,256]{2,1,0:T(4,128)(2,1)S(1)}, u32[]{:S(2)}, u32[]{:S(2)}) collective-permute-start(bf16[3,4,256]{2,1,0:T(4,128)(2,1)S(1)} %get-tuple-element.44), channel_id=1, source_target_pairs={{0,16},{8,48},{16,80},{24,112},{32,144},{40,176},{48,208},{56,240}... | collective-permute-start | bytes 18440 | tf_op jit(solution)/shard_map/ppermute | solution.py:175
  162.0 34.5 %collective-permute-start.7 = (bf16[3,4,256]{2,1,0:T(4,128)(2,1)S(1)}, bf16[3,4,256]{2,1,0:T(4,128)(2,1)S(1)}, u32[]{:S(2)}, u32[]{:S(2)}) collective-permute-start(bf16[3,4,256]{2,1,0:T(4,128)(2,1)S(1)} %get-tuple-element.45), channel_id=1, source_target_pairs={{0,8},{8,40},{16,72},{24,104},{32,136},{40,168},{48,200},{56,232},... | collective-permute-start | bytes 18440 | tf_op jit(solution)/shard_map/ppermute | solution.py:175
  196.5 3.3 %collective-permute-start.6 = (bf16[3,4,256]{2,1,0:T(4,128)(2,1)S(1)}, bf16[3,4,256]{2,1,0:T(4,128)(2,1)S(1)}, u32[]{:S(2)}, u32[]{:S(2)}) collective-permute-start(bf16[3,4,256]{2,1,0:T(4,128)(2,1)S(1)} %get-tuple-element.42), channel_id=1, source_target_pairs={{0,0},{8,32},{16,64},{24,96},{32,128},{40,160},{48,192},{56,224},{... | collective-permute-start | bytes 18440 | tf_op jit(solution)/shard_map/ppermute | solution.py:175
  199.8 4.0 %collective-permute-done.6 = bf16[3,4,256]{2,1,0:T(4,128)(2,1)S(1)} collective-permute-done((bf16[3,4,256]{2,1,0:T(4,128)(2,1)S(1)}, bf16[3,4,256]{2,1,0:T(4,128)(2,1)S(1)}, u32[]{:S(2)}, u32[]{:S(2)}) %collective-permute-start.6) | collective-permute-done | bytes 6176 | tf_op jit(solution)/shard_map/ppermute | solution.py:175
  203.9 7.5 %convolution_convert_fusion.1 = bf16[768,512]{0,1:T(8,128)(2,1)S(1)} fusion(bf16[768,4096]{0,1:T(8,128)(2,1)} %bitcast.91, bf16[4096,512]{1,0:T(8,128)(2,1)} %all-gather.2.cloned.1.call-done), kind=kOutput, calls=%fused_computation.8 | convolution fusion | flops 3221618688 | bytes 11272192 | tf_op jit(solution)/shard_map/dot_general | solution.py:91
  212.3 1.9 collective-permute-start.13
  214.2 3.4 %collective-permute-start.12 = (bf16[3,4,256]{2,1,0:T(4,128)(2,1)S(1)}, bf16[3,4,256]{2,1,0:T(4,128)(2,1)S(1)}, u32[]{:S(2)}, u32[]{:S(2)}) collective-permute-start(bf16[3,4,256]{2,1,0:T(4,128)(2,1)S(1)} %squeeze.123), channel_id=1, source_target_pairs={{16,0},{48,8},{80,16},{112,24},{144,32},{176,40},{208,48},{240,56}... | collective-permute-start | bytes 18440 | tf_op jit(solution)/shard_map/ppermute | solution.py:186
  217.6 4.2 %collective-permute-start.11 = (bf16[3,4,256]{2,1,0:T(4,128)(2,1)S(1)}, bf16[3,4,256]{2,1,0:T(4,128)(2,1)S(1)}, u32[]{:S(2)}, u32[]{:S(2)}) collective-permute-start(bf16[3,4,256]{2,1,0:T(4,128)(2,1)S(1)} %squeeze.122), channel_id=1, source_target_pairs={{8,0},{40,8},{72,16},{104,24},{136,32},{168,40},{200,48},{232,56},... | collective-permute-start | bytes 18440 | tf_op jit(solution)/shard_map/ppermute | solution.py:186
  221.9 3.7 %collective-permute-start.10 = (bf16[3,4,256]{2,1,0:T(4,128)(2,1)S(1)}, bf16[3,4,256]{2,1,0:T(4,128)(2,1)S(1)}, u32[]{:S(2)}, u32[]{:S(2)}) collective-permute-start(bf16[3,4,256]{2,1,0:T(4,128)(2,1)S(1)} %squeeze.121), channel_id=1, source_target_pairs={{0,0},{32,8},{64,16},{96,24},{128,32},{160,40},{192,48},{224,56},{... | collective-permute-start | bytes 18440 | tf_op jit(solution)/shard_map/ppermute | solution.py:186
  225.6 4.8 %collective-permute-done.10 = bf16[3,4,256]{2,1,0:T(4,128)(2,1)S(1)} collective-permute-done((bf16[3,4,256]{2,1,0:T(4,128)(2,1)S(1)}, bf16[3,4,256]{2,1,0:T(4,128)(2,1)S(1)}, u32[]{:S(2)}, u32[]{:S(2)}) %collective-permute-start.10) | collective-permute-done | bytes 6176 | tf_op jit(solution)/shard_map/ppermute | solution.py:186
  (145 shorter events, 21.2 us)
Async XLA Ops:
  8.0 50.7 %copy-start = (bf16[256,4096]{1,0:T(8,128)(2,1)S(1)}, bf16[256,4096]{1,0:T(8,128)(2,1)}, u32[]{:S(2)}) copy-start(bf16[256,4096]{1,0:T(8,128)(2,1)} %param.25) | copy-start | bytes 6291460
  15.3 6.2 %copy-start.11 = (bf16[48,256]{1,0:T(8,128)(2,1)}, bf16[48,256]{1,0:T(8,128)(2,1)S(1)}, u32[]{:S(2)}) copy-start(bf16[48,256]{1,0:T(8,128)(2,1)S(1)} %convolution_convert_fusion.5) | copy-start | bytes 73732
  16.0 26.8 %collective-permute-start.3 = (bf16[2,3,16,256]{3,2,0,1:T(8,128)(2,1)}, bf16[2,3,16,256]{3,2,0,1:T(8,128)(2,1)}, u32[]{:S(2)}, u32[]{:S(2)}) collective-permute-start(bf16[2,3,16,256]{3,2,0,1:T(8,128)(2,1)} %pad_maximum_fusion.4), channel_id=1, source_target_pairs={{64,0},{72,8},{80,16},{88,24},{96,32},{104,40},{112,48},{120,56},{... | collective-permute-start | bytes 147464 | tf_op jit(solution)/shard_map/ppermute | solution.py:32
  16.1 27.0 %collective-permute-start.4 = (bf16[2,3,16,256]{3,2,0,1:T(8,128)(2,1)}, bf16[2,3,16,256]{3,2,0,1:T(8,128)(2,1)}, u32[]{:S(2)}, u32[]{:S(2)}) collective-permute-start(bf16[2,3,16,256]{3,2,0,1:T(8,128)(2,1)} %pad_maximum_fusion.4), channel_id=1, source_target_pairs={{128,0},{136,8},{144,16},{152,24},{160,32},{168,40},{176,48},{184,... | collective-permute-start | bytes 147464 | tf_op jit(solution)/shard_map/ppermute | solution.py:32
  18.8 24.4 %collective-permute-start.5 = (bf16[2,3,16,256]{3,2,0,1:T(8,128)(2,1)}, bf16[2,3,16,256]{3,2,0,1:T(8,128)(2,1)}, u32[]{:S(2)}, u32[]{:S(2)}) collective-permute-start(bf16[2,3,16,256]{3,2,0,1:T(8,128)(2,1)} %pad_maximum_fusion.4), channel_id=1, source_target_pairs={{192,0},{200,8},{208,16},{216,24},{224,32},{232,40},{240,48},{248,... | collective-permute-start | bytes 147464 | tf_op jit(solution)/shard_map/ppermute | solution.py:32
  20.1 24.8 %collective-permute-start = (bf16[2,16,32,256]{3,1,2,0:T(8,128)(2,1)}, bf16[2,16,32,256]{3,1,2,0:T(8,128)(2,1)}, u32[]{:S(2)}, u32[]{:S(2)}) collective-permute-start(bf16[2,16,32,256]{3,1,2,0:T(8,128)(2,1)} %pad_maximum_fusion.2), channel_id=1, source_target_pairs={{64,0},{72,8},{80,16},{88,24},{96,32},{104,40},{112,48},{120,56},{... | collective-permute-start | bytes 1572872 | tf_op jit(solution)/shard_map/ppermute | solution.py:32
  21.5 23.4 %collective-permute-start.1 = (bf16[2,16,32,256]{3,1,2,0:T(8,128)(2,1)}, bf16[2,16,32,256]{3,1,2,0:T(8,128)(2,1)}, u32[]{:S(2)}, u32[]{:S(2)}) collective-permute-start(bf16[2,16,32,256]{3,1,2,0:T(8,128)(2,1)} %pad_maximum_fusion.2), channel_id=1, source_target_pairs={{128,0},{136,8},{144,16},{152,24},{160,32},{168,40},{176,48},{184,... | collective-permute-start | bytes 1572872 | tf_op jit(solution)/shard_map/ppermute | solution.py:32
  27.6 8.4 %copy-start.17 = (s32[3,512]{1,0:T(4,128)S(1)}, s32[3,512]{1,0:T(4,128)}, u32[]{:S(2)}) copy-start(s32[3,512]{1,0:T(4,128)} %param.33) | copy-start | bytes 18436
  27.6 176.3 %all-to-all-start = ((bf16[8,768,512]{1,2,0:T(8,128)(2,1)}), bf16[8,768,512]{1,2,0:T(8,128)(2,1)}, u32[]{:S(2)}, u32[]{:S(2)}) async-start(bf16[8,768,512]{1,2,0:T(8,128)(2,1)} %stack.86), calls=%async_computation | async-start | bytes 12582912 | tf_op jit(solution)/shard_map/all_to_all | solution.py:82
  35.9 114.7 %all-reduce.2.cloned.1.call-start = ((), (), s32[]{:S(2)}) async-start(), calls=%async_computation.1 | async-start | bytes 786432 | tf_op jit(solution)/shard_map/psum | solution.py:160
  39.1 15.2 %copy-start.3 = (bf16[1,16,32,256]{3,1,2,0:T(8,128)(2,1)S(1)}, bf16[1,16,32,256]{3,1,2,0:T(8,128)(2,1)}, u32[]{:S(2)}) copy-start(bf16[1,16,32,256]{3,1,2,0:T(8,128)(2,1)} %copy-done.2) | copy-start | bytes 786436
  39.1 15.2 %copy-start.5 = (bf16[1,16,32,256]{3,1,2,0:T(8,128)(2,1)S(1)}, bf16[1,16,32,256]{3,1,2,0:T(8,128)(2,1)}, u32[]{:S(2)}) copy-start(bf16[1,16,32,256]{3,1,2,0:T(8,128)(2,1)} %copy-done.4) | copy-start | bytes 786436
  42.8 11.5 %collective-permute-start.2 = (bf16[2,16,32,256]{3,1,2,0:T(8,128)(2,1)}, bf16[2,16,32,256]{3,1,2,0:T(8,128)(2,1)S(1)}, u32[]{:S(2)}, u32[]{:S(2)}) collective-permute-start(bf16[2,16,32,256]{3,1,2,0:T(8,128)(2,1)} %pad_maximum_fusion.2), channel_id=1, source_target_pairs={{192,0},{200,8},{208,16},{216,24},{224,32},{232,40},{240,48},{248,... | collective-permute-start | bytes 1572872 | tf_op jit(solution)/shard_map/ppermute | solution.py:32
  57.7 92.9 %copy-start.1 = (bf16[3,16,4096]{2,1,0:T(8,128)(2,1)S(1)}, bf16[3,16,4096]{2,1,0:T(8,128)(2,1)}, u32[]{:S(2)}) copy-start(bf16[3,16,4096]{2,1,0:T(8,128)(2,1)} %param.18) | copy-start | bytes 1179652
  58.7 93.3 %copy-start.16 = (f32[4096]{0:T(1024)S(1)}, f32[4096]{0:T(1024)}, u32[]{:S(2)}) copy-start(f32[4096]{0:T(1024)} %param.26) | copy-start | bytes 49156
  60.0 143.9 %all-gather.2.cloned.1.call-start = ((), (), s32[]{:S(2)}) async-start(), calls=%async_computation.2 | async-start | bytes 4325376 | tf_op jit(solution)/shard_map/all_gather | solution.py:80
  153.7 46.1 %collective-permute-start.9 = (bf16[3,4,256]{2,1,0:T(4,128)(2,1)S(1)}, bf16[3,4,256]{2,1,0:T(4,128)(2,1)S(1)}, u32[]{:S(2)}, u32[]{:S(2)}) collective-permute-start(bf16[3,4,256]{2,1,0:T(4,128)(2,1)S(1)} %get-tuple-element.43), channel_id=1, source_target_pairs={{0,24},{8,56},{16,88},{24,120},{32,152},{40,184},{48,216},{56,248}... | collective-permute-start | bytes 18440 | tf_op jit(solution)/shard_map/ppermute | solution.py:175
  159.3 40.5 %collective-permute-start.8 = (bf16[3,4,256]{2,1,0:T(4,128)(2,1)S(1)}, bf16[3,4,256]{2,1,0:T(4,128)(2,1)S(1)}, u32[]{:S(2)}, u32[]{:S(2)}) collective-permute-start(bf16[3,4,256]{2,1,0:T(4,128)(2,1)S(1)} %get-tuple-element.44), channel_id=1, source_target_pairs={{0,16},{8,48},{16,80},{24,112},{32,144},{40,176},{48,208},{56,240}... | collective-permute-start | bytes 18440 | tf_op jit(solution)/shard_map/ppermute | solution.py:175
  162.0 37.9 %collective-permute-start.7 = (bf16[3,4,256]{2,1,0:T(4,128)(2,1)S(1)}, bf16[3,4,256]{2,1,0:T(4,128)(2,1)S(1)}, u32[]{:S(2)}, u32[]{:S(2)}) collective-permute-start(bf16[3,4,256]{2,1,0:T(4,128)(2,1)S(1)} %get-tuple-element.45), channel_id=1, source_target_pairs={{0,8},{8,40},{16,72},{24,104},{32,136},{40,168},{48,200},{56,232},... | collective-permute-start | bytes 18440 | tf_op jit(solution)/shard_map/ppermute | solution.py:175
  196.5 7.4 %collective-permute-start.6 = (bf16[3,4,256]{2,1,0:T(4,128)(2,1)S(1)}, bf16[3,4,256]{2,1,0:T(4,128)(2,1)S(1)}, u32[]{:S(2)}, u32[]{:S(2)}) collective-permute-start(bf16[3,4,256]{2,1,0:T(4,128)(2,1)S(1)} %get-tuple-element.42), channel_id=1, source_target_pairs={{0,0},{8,32},{16,64},{24,96},{32,128},{40,160},{48,192},{56,224},{... | collective-permute-start | bytes 18440 | tf_op jit(solution)/shard_map/ppermute | solution.py:175
  212.3 13.3 %collective-permute-start.13 = (bf16[3,4,256]{2,1,0:T(4,128)(2,1)S(1)}, bf16[3,4,256]{2,1,0:T(4,128)(2,1)S(1)}, u32[]{:S(2)}, u32[]{:S(2)}) collective-permute-start(bf16[3,4,256]{2,1,0:T(4,128)(2,1)S(1)} %squeeze.124), channel_id=1, source_target_pairs={{24,0},{56,8},{88,16},{120,24},{152,32},{184,40},{216,48},{248,56}... | collective-permute-start | bytes 18440 | tf_op jit(solution)/shard_map/ppermute | solution.py:186
  214.2 11.4 %collective-permute-start.12 = (bf16[3,4,256]{2,1,0:T(4,128)(2,1)S(1)}, bf16[3,4,256]{2,1,0:T(4,128)(2,1)S(1)}, u32[]{:S(2)}, u32[]{:S(2)}) collective-permute-start(bf16[3,4,256]{2,1,0:T(4,128)(2,1)S(1)} %squeeze.123), channel_id=1, source_target_pairs={{16,0},{48,8},{80,16},{112,24},{144,32},{176,40},{208,48},{240,56}... | collective-permute-start | bytes 18440 | tf_op jit(solution)/shard_map/ppermute | solution.py:186
  217.6 8.0 %collective-permute-start.11 = (bf16[3,4,256]{2,1,0:T(4,128)(2,1)S(1)}, bf16[3,4,256]{2,1,0:T(4,128)(2,1)S(1)}, u32[]{:S(2)}, u32[]{:S(2)}) collective-permute-start(bf16[3,4,256]{2,1,0:T(4,128)(2,1)S(1)} %squeeze.122), channel_id=1, source_target_pairs={{8,0},{40,8},{72,16},{104,24},{136,32},{168,40},{200,48},{232,56},... | collective-permute-start | bytes 18440 | tf_op jit(solution)/shard_map/ppermute | solution.py:186
  221.9 8.6 %collective-permute-start.10 = (bf16[3,4,256]{2,1,0:T(4,128)(2,1)S(1)}, bf16[3,4,256]{2,1,0:T(4,128)(2,1)S(1)}, u32[]{:S(2)}, u32[]{:S(2)}) collective-permute-start(bf16[3,4,256]{2,1,0:T(4,128)(2,1)S(1)} %squeeze.121), channel_id=1, source_target_pairs={{0,0},{32,8},{64,16},{96,24},{128,32},{160,40},{192,48},{224,56},{... | collective-permute-start | bytes 18440 | tf_op jit(solution)/shard_map/ppermute | solution.py:186
  (11 other events, 41.6 us)
Sparse Core Ops, SparseCore 0:
  60.1 90.4 all-reduce.1
Sparse Core Ops, SparseCore 1:
  63.0 54.0 all-gather.1
